TPU v7x, 256 devices: a whole 4x4x8 slice. The times are simulated.
256 devices in a mesh: row: 32 (over x, y, core), col: 8 (over z).
Axes of the slice: x: 4, y: 4, z: 8, core: 2. Of those that a mesh axis runs over, the one named last changes fastest.
Arguments:
- matrix: float32 [16384, 16384], P('row', 'col'), may hold values from -9 to 9
- vectors: float32 [16384, 128], P('row'), may hold values from -0.125 to 0.125
- tfactor: float32 [128, 128], replicated, may hold values from -1 to 2, as said below
Outputs:
- updated: float32 [16384, 16384], P('row', 'col')
Inputs may be any that keep to these rules, and one draw needn't show every extreme that they name: tfactor is upper triangular with its diagonal between 0.7 and 1.4.
All inputs are finite; a program needn't handle non-finite values.
Results may differ from a plain program's by a relative error of at most 0.000094.
Values sent between devices are 32-bit elements; how exact they have to be, the bound alone decides.
No kernel may reach another device: no remote copies, remote signals or barrier semaphores. Data moves between devices by JAX's collectives and lax.ppermute only.
A program may use at most 128 MiB of HBM per device.

v0:
```python
import jax
import jax.numpy as jnp
from jax import lax
from jax.sharding import PartitionSpec as P


def product(left, right):
    return jnp.dot(left, right, precision=lax.Precision.HIGHEST, preferred_element_type=jnp.float32)


def inner_product(left, right):
    return lax.dot_general(
        left,
        right,
        (((0,), (0,)), ((), ())),
        precision=lax.Precision.HIGHEST,
        preferred_element_type=jnp.float32,
    )


def outer_product(left, right):
    return lax.dot_general(
        left,
        right,
        (((1,), (1,)), ((), ())),
        precision=lax.Precision.HIGHEST,
        preferred_element_type=jnp.float32,
    )


def to_columns(panel_rows):
    rows_here = panel_rows.shape[0]
    row_count = lax.axis_size("row")
    blocks_per = row_count // lax.axis_size("col")
    col_index = lax.axis_index("col")
    gathered = lax.all_gather(panel_rows, "row", axis=0, tiled=True)
    return lax.dynamic_slice_in_dim(
        gathered, col_index * (blocks_per * rows_here), blocks_per * rows_here, 0
    )


def shards(matrix, vectors, tfactor):
    vec_cols = to_columns(vectors)
    x_rows = lax.psum(product(matrix, vec_cols), "col")
    y_rows = product(x_rows, tfactor)
    cross_terms = lax.psum(inner_product(vectors, y_rows), "row")
    coupling = inner_product(tfactor, cross_terms)
    w_rows = y_rows - 0.5 * product(vectors, coupling)
    w_cols = to_columns(w_rows)
    return matrix - outer_product(vectors, w_cols) - outer_product(w_rows, vec_cols)


def solution(mesh):
    in_specs = (P("row", "col"), P("row", None), P())
    out_specs = P("row", "col")
    return jax.shard_map(shards, mesh=mesh, in_specs=in_specs, out_specs=out_specs, check_vma=False)
```

profile of v0, /device:TPU:1, one launch (start us, length us, event | category | flops | bytes accessed | tf_op | source)
XLA Modules:
  0.0 338.5 jit_solution(5405151360092062463)
XLA Ops:
  6.5 0.0 copy-start
  6.5 0.0 copy-start.1
  6.5 0.0 all-gather.3.cloned.1.call-start
  6.5 0.7 all-gather.3.cloned.1.call-update
  7.3 0.0 all-reduce.3.cloned.1.call-start
  7.3 64.8 %all-gather.3.cloned.1.call-done = f32[16384,128]{1,0:T(8,128)} async-done(((f32[512,128]{1,0:T(8,128)}), f32[16384,128]{1,0:T(8,128)}) %all-gather.3.cloned.1.call-update) | async-done | bytes 8388624 | tf_op jit(solution)/shard_map/all_gather | solution.py:36
  72.1 7.7 %convolution_bitcast_fusion = f32[512,128]{0,1:T(8,128)} fusion(f32[512,2048]{1,0:T(8,128)} %param.3, f32[16384,128]{1,0:T(8,128)} %all-gather.3.cloned.1.call-done, s32[]{:T(128)S(6)} %select_n.4), kind=kOutput, calls=%fused_computation.5 | convolution fusion | flops 1610612736 | bytes 5505028 | tf_op jit(solution)/shard_map/dot_general | solution.py:8
  79.7 0.0 all-reduce.3.cloned.1.call-update
  79.8 0.0 all-reduce.5.cloned.1.call-start
  79.8 67.3 %all-reduce.3.cloned.1.call-done = f32[512,128]{0,1:T(8,128)} async-done(((f32[512,128]{0,1:T(8,128)}), f32[512,128]{0,1:T(8,128)}) %all-reduce.3.cloned.1.call-update) | async-done | bytes 262160 | tf_op jit(solution)/shard_map/psum | solution.py:44
  147.1 0.0 copy-done
  147.1 1.5 fusion.10
  148.6 0.0 copy-done.1
  148.7 1.2 convolution_bitcast_fusion.1
  149.9 0.0 all-reduce.5.cloned.1.call-update
  149.9 0.0 all-gather.5.cloned.1.call-start
  150.0 109.7 %all-reduce.5.cloned.1.call-done = f32[128,128]{0,1:T(8,128)} async-done(((f32[128,128]{0,1:T(8,128)}), f32[128,128]{0,1:T(8,128)}) %all-reduce.5.cloned.1.call-update) | async-done | bytes 65552 | tf_op jit(solution)/shard_map/psum | solution.py:46
  259.7 1.0 fusion.11
  260.7 1.1 fusion.2
  261.8 0.0 all-gather.5.cloned.1.call-update
  261.8 0.0 copy-start.2
  261.8 5.4 %copy.5 = f32[512,2048]{0,1:T(8,128)} copy(f32[512,2048]{1,0:T(8,128)} %param.3) | data formatting | bytes 8388608 | tf_op args[0]
  267.2 0.0 copy-done.2
  267.2 6.2 %fusion.4 = f32[512,2048]{0,1:T(8,128)} fusion(f32[512,128]{1,0:T(8,128)S(1)} %copy-done.2, f32[16384,128]{1,0:T(8,128)} %all-gather.3.cloned.1.call-done, s32[]{:T(128)S(6)} %select_n.4), kind=kOutput, calls=%fused_computation.8 | convolution fusion | flops 1610612736 | bytes 5505028 | tf_op jit(solution)/shard_map/dot_general | solution.py:22
  273.4 45.7 %all-gather.5.cloned.1.call-done = f32[16384,128]{1,0:T(8,128)} async-done(((f32[512,128]{1,0:T(8,128)}), f32[16384,128]{1,0:T(8,128)}) %all-gather.5.cloned.1.call-update) | async-done | bytes 8388624 | tf_op jit(solution)/shard_map/all_gather | solution.py:36
  319.1 7.5 %fusion = f32[512,2048]{0,1:T(8,128)} fusion(f32[512,2048]{0,1:T(8,128)} %fusion.4, f32[512,2048]{0,1:T(8,128)} %copy.5, f32[512,128]{1,0:T(8,128)S(1)} %copy-done.1, f32[16384,128]{1,0:T(8,128)} %all-gather.5.cloned.1.call-done, s32[]{:T(128)S(6)} %select_n.4), kind=kOutput, calls=%fused_computation.1 | convolution fusion | flops 1612709888 | bytes 13893636 | tf_op jit(solution)/shard_map/dot_general | solution.py:22
  326.6 5.3 %copy.7 = f32[512,2048]{1,0:T(8,128)} copy(f32[512,2048]{0,1:T(8,128)} %fusion) | data formatting | bytes 8388608 | tf_op jit(solution)/shard_map/sub | solution.py:50
Async XLA Ops:
  6.5 140.6 %copy-start = (f32[128,128]{1,0:T(8,128)S(1)}, f32[128,128]{1,0:T(8,128)}, u32[]{:S(2)}) copy-start(f32[128,128]{1,0:T(8,128)} %param.5) | copy-start | bytes 196612
  6.5 142.1 %copy-start.1 = (f32[512,128]{1,0:T(8,128)S(1)}, f32[512,128]{1,0:T(8,128)}, u32[]{:S(2)}) copy-start(f32[512,128]{1,0:T(8,128)} %param.4) | copy-start | bytes 786436
  6.5 65.5 %all-gather.3.cloned.1.call-start = ((), (), s32[]{:S(2)}) async-start(), calls=%async_computation | async-start | bytes 8650752 | tf_op jit(solution)/shard_map/all_gather | solution.py:36
  7.3 139.8 %all-reduce.3.cloned.1.call-start = ((), (), s32[]{:S(2)}) async-start(), calls=%async_computation.1 | async-start | bytes 524288 | tf_op jit(solution)/shard_map/psum | solution.py:44
  79.8 179.9 %all-reduce.5.cloned.1.call-start = ((), (), s32[]{:S(2)}) async-start(), calls=%async_computation.2 | async-start | bytes 131072 | tf_op jit(solution)/shard_map/psum | solution.py:46
  149.9 169.2 %all-gather.5.cloned.1.call-start = ((), (), s32[]{:S(2)}) async-start(), calls=%async_computation.3 | async-start | bytes 8650752 | tf_op jit(solution)/shard_map/all_gather | solution.py:36
  261.8 5.4 %copy-start.2 = (f32[512,128]{1,0:T(8,128)S(1)}, f32[512,128]{1,0:T(8,128)}, u32[]{:S(2)}) copy-start(f32[512,128]{1,0:T(8,128)} %fusion.2) | copy-start | bytes 786436
Sparse Core Ops, SparseCore 0:
  9.9 62.1 all-gather.2
  79.9 67.1 all-reduce.2
  150.7 108.9 all-reduce.4
  262.1 56.9 all-gather.4
where the time goes:
time: 339 us
  waiting for transfers between devices  288 us (85%)
  matrix products  26.2 us (8%)
  between operations  13.2 us (4%)
  local copies, waits for them, and re-layouts  10.8 us (3%)
    all_gather x2, waiting for transfers between devices, to_columns(): gathered = lax.all_gather(panel_rows, 'row', axis=0, tiled=True)  110 us
    psum x1, waiting for transfers between devices, shards(): cross_terms = lax.psum(inner_product(vectors, y_rows), 'row')  110 us
    psum x1, waiting for transfers between devices, shards(): x_rows = lax.psum(product(matrix, vec_cols), 'col')  67.3 us
    dot_general x2, matrix products, outer_product(): lax.dot_general(left, right, (((1,), (1,)), ((), ())), precision=lax.Prec...  13.7 us
    dot_general x3, matrix products, product(): jnp.dot(left, right, precision=lax.Precision.HIGHEST, preferred_element_t...  10.3 us
  transfers between devices with their start and end apart: 4, of which 4 were waited for; matrix products, arithmetic and copies ran while one was open for 3% of the time, Pallas kernels for 0%

commit v1 on v0

--- a/solution.py
+++ b/solution.py
@@ -33,7 +33,19 @@
     row_count = lax.axis_size("row")
     blocks_per = row_count // lax.axis_size("col")
     col_index = lax.axis_index("col")
-    gathered = lax.all_gather(panel_rows, "row", axis=0, tiled=True)
+
+    def lift_flows_in(xin):
+        return jnp.concatenate(
+            lax.all_to_all(
+                jnp.stack(lax.axis_size("row") * [xin], axis=0),
+                axis_name="row",
+                split_axis=0,
+                concat_axis=0,
+            ),
+            axis=0,
+        )
+
+    gathered = lift_flows_in(panel_rows)
     return lax.dynamic_slice_in_dim(
         gathered, col_index * (blocks_per * rows_here), blocks_per * rows_here, 0
     )

time: 339 us -> 489 us (1.44)
  the two profiles are of different devices: /device:TPU:1 before, /device:TPU:44 now
where the time goes in v1:
time: 489 us
  waiting for transfers between devices  416 us (85%)
  matrix products  25.5 us (5%)
  local copies, waits for them, and re-layouts  20.1 us (4%)
  starting transfers between devices  13.8 us (3%)
  between operations  13.5 us (3%)
    all_to_all x2, waiting for transfers between devices, lift_flows_in(): lax.all_to_all(jnp.stack(lax.axis_size('row') * [xin], axis=0), axis_name...  239 us
    psum x1, waiting for transfers between devices, shards(): cross_terms = lax.psum(inner_product(vectors, y_rows), 'row')  104 us
    psum x1, waiting for transfers between devices, shards(): x_rows = lax.psum(product(matrix, vec_cols), 'col')  73.3 us
    all_to_all x2, starting transfers between devices, lift_flows_in(): lax.all_to_all(jnp.stack(lax.axis_size('row') * [xin], axis=0), axis_name...  13.7 us
    dot_general x2, matrix products, outer_product(): lax.dot_general(left, right, (((1,), (1,)), ((), ())), precision=lax.Prec...  13.6 us
  transfers between devices with their start and end apart: 4, of which 4 were waited for; matrix products, arithmetic and copies ran while one was open for 2% of the time, Pallas kernels for 0%

profile of v1, /device:TPU:44, one launch (start us, length us, event | category | flops | bytes accessed | tf_op | source)
XLA Modules:
  0.0 488.9 jit_solution(15407347782724344737)
XLA Ops:
  6.5 0.0 copy-start
  6.5 5.2 %stack.4 = f32[32,512,128]{2,1,0:T(8,128)} broadcast(f32[512,128]{1,0:T(8,128)} %param.4), dimensions={1,2} | broadcast | bytes 8650752 | tf_op jit(solution)/shard_map/stack | solution.py:40
  11.7 7.5 %all-to-all-start = ((f32[32,512,128]{2,1,0:T(8,128)}), f32[32,512,128]{2,1,0:T(8,128)}, u32[]{:S(2)}, u32[]{:S(2)}) async-start(f32[32,512,128]{2,1,0:T(8,128)} %stack.4), calls=%async_computation | async-start | bytes 16777216 | tf_op jit(solution)/shard_map/all_to_all | solution.py:39
  19.2 0.0 copy-start.1
  19.3 0.0 all-reduce.3.cloned.1.call-start
  19.3 124.0 %all-to-all-done = f32[32,512,128]{2,1,0:T(8,128)} async-done(((f32[32,512,128]{2,1,0:T(8,128)}), f32[32,512,128]{2,1,0:T(8,128)}, u32[]{:S(2)}, u32[]{:S(2)}) %all-to-all-start) | async-done | bytes 8388640 | tf_op jit(solution)/shard_map/all_to_all | solution.py:39
  143.3 7.7 %convolution_bitcast_fusion = f32[512,128]{0,1:T(8,128)} fusion(f32[512,2048]{1,0:T(8,128)} %param.3, f32[16384,128]{1,0:T(8,128)} %bitcast, s32[]{:T(128)S(6)} %select_n.4), kind=kOutput, calls=%fused_computation.5 | convolution fusion | flops 1610612736 | bytes 5505028 | tf_op jit(solution)/shard_map/dot_general | solution.py:8
  151.0 0.0 all-reduce.3.cloned.1.call-update
  151.0 0.0 all-reduce.5.cloned.1.call-start
  151.1 73.3 %all-reduce.3.cloned.1.call-done = f32[512,128]{0,1:T(8,128)} async-done(((f32[512,128]{0,1:T(8,128)}), f32[512,128]{0,1:T(8,128)}) %all-reduce.3.cloned.1.call-update) | async-done | bytes 262160 | tf_op jit(solution)/shard_map/psum | solution.py:56
  224.3 0.0 copy-done
  224.3 1.5 fusion.10
  225.9 0.0 copy-done.1
  225.9 1.2 convolution_bitcast_fusion.1
  227.1 0.0 all-reduce.5.cloned.1.call-update
  227.1 104.3 %all-reduce.5.cloned.1.call-done = f32[128,128]{0,1:T(8,128)} async-done(((f32[128,128]{0,1:T(8,128)}), f32[128,128]{0,1:T(8,128)}) %all-reduce.5.cloned.1.call-update) | async-done | bytes 65552 | tf_op jit(solution)/shard_map/psum | solution.py:58
  331.5 1.0 fusion.11
  332.5 0.4 fusion.2
  332.9 4.2 stack.5
  337.1 6.1 %all-to-all-start.1 = ((f32[32,512,128]{2,1,0:T(8,128)}), f32[32,512,128]{2,1,0:T(8,128)}, u32[]{:S(2)}, u32[]{:S(2)}) async-start(f32[32,512,128]{2,1,0:T(8,128)} %stack.5), calls=%async_computation.1 | async-start | bytes 16777216 | tf_op jit(solution)/shard_map/all_to_all | solution.py:39
  343.2 5.4 %copy.5 = f32[512,2048]{0,1:T(8,128)} copy(f32[512,2048]{1,0:T(8,128)} %param.3) | data formatting | bytes 8388608 | tf_op args[0]
  348.6 6.2 %fusion.4 = f32[512,2048]{0,1:T(8,128)} fusion(f32[512,128]{1,0:T(8,128)S(1)} %fusion.2, f32[16384,128]{1,0:T(8,128)} %bitcast, s32[]{:T(128)S(6)} %select_n.4), kind=kOutput, calls=%fused_computation.8 | convolution fusion | flops 1610612736 | bytes 5505028 | tf_op jit(solution)/shard_map/dot_general | solution.py:22
  354.8 114.5 %all-to-all-done.1 = f32[32,512,128]{2,1,0:T(8,128)} async-done(((f32[32,512,128]{2,1,0:T(8,128)}), f32[32,512,128]{2,1,0:T(8,128)}, u32[]{:S(2)}, u32[]{:S(2)}) %all-to-all-start.1) | async-done | bytes 8388640 | tf_op jit(solution)/shard_map/all_to_all | solution.py:39
  469.2 7.5 %fusion = f32[512,2048]{0,1:T(8,128)} fusion(f32[512,2048]{0,1:T(8,128)} %fusion.4, f32[512,2048]{0,1:T(8,128)} %copy.5, f32[512,128]{1,0:T(8,128)S(1)} %copy-done.1, f32[16384,128]{1,0:T(8,128)} %bitcast.4, s32[]{:T(128)S(6)} %select_n.4), kind=kOutput, calls=%fused_computation.1 | convolution fusion | flops 1612709888 | bytes 13893636 | tf_op jit(solution)/shard_map/dot_general | solution.py:22
  476.7 5.3 %copy.7 = f32[512,2048]{1,0:T(8,128)} copy(f32[512,2048]{0,1:T(8,128)} %fusion) | data formatting | bytes 8388608 | tf_op jit(solution)/shard_map/sub | solution.py:62
Async XLA Ops:
  6.5 217.8 %copy-start = (f32[128,128]{1,0:T(8,128)S(1)}, f32[128,128]{1,0:T(8,128)}, u32[]{:S(2)}) copy-start(f32[128,128]{1,0:T(8,128)} %param.5) | copy-start | bytes 196612
  11.7 131.6 %all-to-all-start = ((f32[32,512,128]{2,1,0:T(8,128)}), f32[32,512,128]{2,1,0:T(8,128)}, u32[]{:S(2)}, u32[]{:S(2)}) async-start(f32[32,512,128]{2,1,0:T(8,128)} %stack.4), calls=%async_computation | async-start | bytes 16777216 | tf_op jit(solution)/shard_map/all_to_all | solution.py:39
  19.2 206.6 %copy-start.1 = (f32[512,128]{1,0:T(8,128)S(1)}, f32[512,128]{1,0:T(8,128)}, u32[]{:S(2)}) copy-start(f32[512,128]{1,0:T(8,128)} %param.4) | copy-start | bytes 786436
  19.3 205.1 %all-reduce.3.cloned.1.call-start = ((), (), s32[]{:S(2)}) async-start(), calls=%async_computation.2 | async-start | bytes 524288 | tf_op jit(solution)/shard_map/psum | solution.py:56
  151.0 180.4 %all-reduce.5.cloned.1.call-start = ((), (), s32[]{:S(2)}) async-start(), calls=%async_computation.3 | async-start | bytes 131072 | tf_op jit(solution)/shard_map/psum | solution.py:58
  337.1 132.2 %all-to-all-start.1 = ((f32[32,512,128]{2,1,0:T(8,128)}), f32[32,512,128]{2,1,0:T(8,128)}, u32[]{:S(2)}, u32[]{:S(2)}) async-start(f32[32,512,128]{2,1,0:T(8,128)} %stack.5), calls=%async_computation.1 | async-start | bytes 16777216 | tf_op jit(solution)/shard_map/all_to_all | solution.py:39
Sparse Core Ops, SparseCore 0:
  151.1 73.1 all-reduce.2
  227.9 103.4 all-reduce.4

commit v2 on v0

--- a/solution.py
+++ b/solution.py
@@ -43,7 +43,8 @@
     vec_cols = to_columns(vectors)
     x_rows = lax.psum(product(matrix, vec_cols), "col")
     y_rows = product(x_rows, tfactor)
-    cross_terms = lax.psum(inner_product(vectors, y_rows), "row")
+    expand_area = lambda array_here: jnp.sum(lax.all_gather(array_here, "row"), axis=0)
+    cross_terms = expand_area(inner_product(vectors, y_rows))
     coupling = inner_product(tfactor, cross_terms)
     w_rows = y_rows - 0.5 * product(vectors, coupling)
     w_cols = to_columns(w_rows)

time: 339 us -> 284 us (0.84)
  waiting for transfers between devices: 288 us -> 232 us
    psum x1 -> x0, waiting for transfers between devices: 110 us -> none  [shards(): cross_terms = lax.psum(inner_product(vectors, y_rows), 'row')]
    all_gather x0 -> x1, waiting for transfers between devices: none -> 53.2 us  [shards(): lax.all_gather(array_here, 'row')]
    unnamed x7 -> x8, local copies, waits for them, and re-layouts: 5.43 us -> 7.38 us
  transfers between devices with their start and end apart: 4 -> 4, of which waited for: 4 -> 4; matrix products, arithmetic and copies ran while one was open for 3% -> 4% of each run, Pallas kernels for 0% -> 0%
where the time goes in v2:
time: 284 us
  waiting for transfers between devices  232 us (82%)
  matrix products  25.4 us (9%)
  between operations  13.2 us (5%)
  local copies, waits for them, and re-layouts  12.7 us (4%)
    all_gather x2, waiting for transfers between devices, to_columns(): gathered = lax.all_gather(panel_rows, 'row', axis=0, tiled=True)  111 us
    psum x1, waiting for transfers between devices, shards(): x_rows = lax.psum(product(matrix, vec_cols), 'col')  67.3 us
    all_gather x1, waiting for transfers between devices, shards(): lax.all_gather(array_here, 'row')  53.2 us
    dot_general x2, matrix products, outer_product(): lax.dot_general(left, right, (((1,), (1,)), ((), ())), precision=lax.Prec...  13.7 us
    dot_general x3, matrix products, product(): jnp.dot(left, right, precision=lax.Precision.HIGHEST, preferred_element_t...  10.3 us
    unnamed x8, local copies, waits for them, and re-layouts  7.38 us
  transfers between devices with their start and end apart: 4, of which 4 were waited for; matrix products, arithmetic and copies ran while one was open for 4% of the time, Pallas kernels for 0%

profile of v2, /device:TPU:1, one launch (start us, length us, event | category | flops | bytes accessed | tf_op | source)
XLA Modules:
  0.0 283.6 jit_solution(14636713255522737675)
XLA Ops:
  6.5 0.0 copy-start
  6.5 0.0 copy-start.1
  6.5 0.0 all-gather.5.cloned.1.call-start
  6.5 0.7 all-gather.5.cloned.1.call-update
  7.3 0.0 all-reduce.2.cloned.1.call-start
  7.3 64.8 %all-gather.5.cloned.1.call-done = f32[16384,128]{1,0:T(8,128)} async-done(((f32[512,128]{1,0:T(8,128)}), f32[16384,128]{1,0:T(8,128)}) %all-gather.5.cloned.1.call-update) | async-done | bytes 8388624 | tf_op jit(solution)/shard_map/all_gather | solution.py:36
  72.1 7.7 %convolution_bitcast_fusion = f32[512,128]{0,1:T(8,128)} fusion(f32[512,2048]{1,0:T(8,128)} %param.3, f32[16384,128]{1,0:T(8,128)} %all-gather.5.cloned.1.call-done, s32[]{:T(128)S(6)} %select_n.4), kind=kOutput, calls=%fused_computation.6 | convolution fusion | flops 1610612736 | bytes 5505028 | tf_op jit(solution)/shard_map/dot_general | solution.py:8
  79.7 0.0 all-reduce.2.cloned.1.call-update
  79.8 0.0 all-gather.9.cloned.1.call-start
  79.8 67.3 %all-reduce.2.cloned.1.call-done = f32[512,128]{0,1:T(8,128)} async-done(((f32[512,128]{0,1:T(8,128)}), f32[512,128]{0,1:T(8,128)}) %all-reduce.2.cloned.1.call-update) | async-done | bytes 262160 | tf_op jit(solution)/shard_map/psum | solution.py:44
  147.1 0.0 copy-done
  147.1 1.5 fusion.10
  148.6 0.0 copy-done.1
  148.7 1.2 convolution_bitcast_fusion.1
  149.9 0.0 all-gather.9.cloned.1.call-update
  149.9 0.0 all-gather.7.cloned.1.call-start
  150.0 53.2 %all-gather.9.cloned.1.call-done = f32[4096,128]{0,1:T(8,128)} async-done(((f32[128,128]{0,1:T(8,128)}), f32[4096,128]{0,1:T(8,128)}) %all-gather.9.cloned.1.call-update) | async-done | bytes 2097168 | tf_op jit(solution)/shard_map/all_gather | solution.py:46
  203.2 2.0 copy.14
  205.1 0.2 bitcast_reduce_fusion
  205.4 0.2 fusion.11
  205.6 1.1 fusion.2
  206.7 0.0 all-gather.7.cloned.1.call-update
  206.7 0.0 copy-start.2
  206.7 5.4 %copy.9 = f32[512,2048]{0,1:T(8,128)} copy(f32[512,2048]{1,0:T(8,128)} %param.3) | data formatting | bytes 8388608 | tf_op args[0]
  212.1 0.0 copy-done.2
  212.1 6.2 %fusion.4 = f32[512,2048]{0,1:T(8,128)} fusion(f32[512,128]{1,0:T(8,128)S(1)} %copy-done.2, f32[16384,128]{1,0:T(8,128)} %all-gather.5.cloned.1.call-done, s32[]{:T(128)S(6)} %select_n.4), kind=kOutput, calls=%fused_computation.9 | convolution fusion | flops 1610612736 | bytes 5505028 | tf_op jit(solution)/shard_map/dot_general | solution.py:22
  218.3 46.0 %all-gather.7.cloned.1.call-done = f32[16384,128]{1,0:T(8,128)} async-done(((f32[512,128]{1,0:T(8,128)}), f32[16384,128]{1,0:T(8,128)}) %all-gather.7.cloned.1.call-update) | async-done | bytes 8388624 | tf_op jit(solution)/shard_map/all_gather | solution.py:36
  264.2 7.5 %fusion = f32[512,2048]{0,1:T(8,128)} fusion(f32[512,2048]{0,1:T(8,128)} %fusion.4, f32[512,2048]{0,1:T(8,128)} %copy.9, f32[512,128]{1,0:T(8,128)S(1)} %copy-done.1, f32[16384,128]{1,0:T(8,128)} %all-gather.7.cloned.1.call-done, s32[]{:T(128)S(6)} %select_n.4), kind=kOutput, calls=%fused_computation.1 | convolution fusion | flops 1612709888 | bytes 13893636 | tf_op jit(solution)/shard_map/dot_general | solution.py:22
  271.8 5.3 %copy.11 = f32[512,2048]{1,0:T(8,128)} copy(f32[512,2048]{0,1:T(8,128)} %fusion) | data formatting | bytes 8388608 | tf_op jit(solution)/shard_map/sub | solution.py:51
Async XLA Ops:
  6.5 140.6 %copy-start = (f32[128,128]{1,0:T(8,128)S(1)}, f32[128,128]{1,0:T(8,128)}, u32[]{:S(2)}) copy-start(f32[128,128]{1,0:T(8,128)} %param.5) | copy-start | bytes 196612
  6.5 142.1 %copy-start.1 = (f32[512,128]{1,0:T(8,128)S(1)}, f32[512,128]{1,0:T(8,128)}, u32[]{:S(2)}) copy-start(f32[512,128]{1,0:T(8,128)} %param.4) | copy-start | bytes 786436
  6.5 65.5 %all-gather.5.cloned.1.call-start = ((), (), s32[]{:S(2)}) async-start(), calls=%async_computation | async-start | bytes 8650752 | tf_op jit(solution)/shard_map/all_gather | solution.py:36
  7.3 139.8 %all-reduce.2.cloned.1.call-start = ((), (), s32[]{:S(2)}) async-start(), calls=%async_computation.1 | async-start | bytes 524288 | tf_op jit(solution)/shard_map/psum | solution.py:44
  79.8 123.4 %all-gather.9.cloned.1.call-start = ((), (), s32[]{:S(2)}) async-start(), calls=%async_computation.3 | async-start | bytes 2162688 | tf_op jit(solution)/shard_map/all_gather | solution.py:46
  149.9 114.3 %all-gather.7.cloned.1.call-start = ((), (), s32[]{:S(2)}) async-start(), calls=%async_computation.2 | async-start | bytes 8650752 | tf_op jit(solution)/shard_map/all_gather | solution.py:36
  206.7 5.4 %copy-start.2 = (f32[512,128]{1,0:T(8,128)S(1)}, f32[512,128]{1,0:T(8,128)}, u32[]{:S(2)}) copy-start(f32[512,128]{1,0:T(8,128)} %fusion.2) | copy-start | bytes 786436
Sparse Core Ops, SparseCore 0:
  9.9 62.1 all-gather.4
  79.9 67.1 all-reduce.1
  150.0 53.1 all-gather.8
  206.8 57.3 all-gather.6
